TPU v7x, 32 devices: a whole 2x2x4 slice. The times are simulated.
32 devices in a mesh: dp: 8 (over z, x), group: 4 (over y, core).
Axes of the slice: x: 2, y: 2, z: 4, core: 2. Of those that a mesh axis runs over, the one named last changes fastest.
Arguments:
- partials: float32 [4, 54, 1024, 1024], P('group', None, 'dp'), may hold values from -0.3 to 0.3
- second_moment: float32 [54, 1024, 1024], P(None, 'dp', 'group'), may hold values from 0.0001 to 0.01
- left_stats: float32 [54, 1024, 1024], P(None, 'dp', 'group'), may hold values from -3 to 3
- right_stats: float32 [54, 1024, 1024], P(None, 'dp', 'group'), may hold values from -3 to 3
- left_roots: bfloat16 [54, 1024, 1024], P(None, 'dp', 'group'), may hold values from -0.2 to 2.1
- right_roots: bfloat16 [54, 1024, 1024], P(None, 'dp', 'group'), may hold values from -0.2 to 2.1
- norm_partials: float32 [8, 4, 2, 2048], P('dp', 'group'), may hold values from -0.012 to 0.012
- norm_moment: float32 [2, 2048], replicated, may hold values from 0.0001 to 0.01
Outputs:
- block_step: bfloat16 [54, 1024, 1024], P(None, 'dp', 'group')
- new_moment: float32 [54, 1024, 1024], P(None, 'dp', 'group')
- new_left: float32 [54, 1024, 1024], P(None, 'dp', 'group')
- new_right: float32 [54, 1024, 1024], P(None, 'dp', 'group')
- norm_step: float32 [2, 2048], replicated
- new_norm_moment: float32 [2, 2048], replicated
All inputs are finite; a program needn't handle non-finite values.
Results may differ from a plain program's by a relative error of at most 0.0042.
The roundings to bfloat16 on the way count: a program that leaves them out, or rounds other values in their place, can miss the bound.
Values may be sent and summed in bfloat16 or wider, within the bound.
No kernel may reach another device: no remote copies, remote signals or barrier semaphores. Data moves between devices by JAX's collectives and lax.ppermute only.
A program may use at most 384 MiB of HBM per device.

v0:
```python
import jax
import jax.numpy as jnp
from jax import lax
from jax.sharding import PartitionSpec as P

EPS_ADAM = 1e-08
EPS_GRAFT = 1e-06


def on_device(
    partials,
    second_moment,
    left_stats,
    right_stats,
    left_roots,
    right_roots,
    norm_partials,
    norm_moment,
):
    n_dp = lax.axis_size("dp")
    me_dp = lax.axis_index("dp")
    me_group = lax.axis_index("group")
    count = second_moment.shape[0]
    rows = partials.shape[2]
    quarter = second_moment.shape[2]
    width = rows * n_dp
    cap = -(-count // n_dp)
    slots = cap * n_dp
    lower = me_group * quarter
    split = (cap + 1) // 2
    bounds = [(0, split), (split, cap)] if cap > 1 else [(0, cap)]

    def to_owners(blocks, n_slots):
        padded = jnp.pad(blocks, ((0, n_slots * n_dp - blocks.shape[0]), (0, 0), (0, 0)))
        sent = lax.all_to_all(padded.reshape(n_slots, n_dp, rows, quarter), "dp", 1, 1, tiled=True)
        return sent.reshape(n_slots, width, quarter)

    def to_keepers(owned):
        n_slots = owned.shape[0]
        back = lax.all_to_all(owned.reshape(n_slots, n_dp, rows, quarter), "dp", 1, 1, tiled=True)
        return back.reshape(n_slots * n_dp, rows, quarter)

    def roots_to_owners(blocks):
        padded = jnp.pad(blocks, ((0, slots - count), (0, 0), (0, 0)))
        return lax.all_to_all(padded.reshape(cap, n_dp, rows, quarter), "dp", 1, 1, tiled=True)

    left_sent = roots_to_owners(left_roots)
    right_sent = roots_to_owners(right_roots)
    local_norm = norm_partials[0, 0]
    grads, moments, adam_parts = ([], [], [])
    for index, (s0, s1) in enumerate(bounds):
        b0, b1 = (s0 * n_dp, min(s1 * n_dp, count))
        grad = lax.psum_scatter(partials[0, b0:b1], "group", scatter_dimension=2, tiled=True)
        low = grad.astype(jnp.bfloat16)
        if index == 0:
            grad, low, left_sent, right_sent = lax.optimization_barrier(
                (grad, low, left_sent, right_sent)
            )
        new_moment = 0.99 * second_moment[b0:b1] + 0.01 * grad * grad
        adam = grad / (jnp.sqrt(new_moment) + EPS_ADAM)
        adam_parts.append(jnp.sum(adam * adam, axis=(1, 2)))
        moments.append(new_moment)
        grads.append(low)
    left_root = left_sent.reshape(cap, width, quarter)
    right_root = right_sent.reshape(cap, width, quarter)
    adam_cat = jnp.pad(jnp.concatenate(adam_parts), (0, slots - count))
    adam_rows = adam_cat.reshape(cap, n_dp).T
    norm_rows = jnp.broadcast_to(local_norm.reshape(1, -1), (n_dp, local_norm.size))
    sent = lax.all_to_all(jnp.concatenate([adam_rows, norm_rows], axis=1), "dp", 0, 0, tiled=True)
    dp_sums = jnp.sum(sent, axis=0)
    left_terms, right_terms, pieces = ([], [], [])
    for (s0, s1), grad_low in zip(bounds, grads):
        b0, b1 = (s0 * n_dp, min(s1 * n_dp, count))
        mine = to_owners(grad_low, s1 - s0)
        piece = lax.all_gather(mine, "group", axis=2, tiled=True)
        if s0 == 0:
            dp_sums, piece = lax.optimization_barrier((dp_sums, piece))
        own_rows = lax.dynamic_slice_in_dim(piece, lower, quarter, 1)
        gram_left = jnp.einsum("cim,cjm->cij", piece, own_rows, preferred_element_type=jnp.float32)
        gram_right = jnp.einsum("cim,cij->cmj", piece, mine, preferred_element_type=jnp.float32)
        both = jnp.concatenate([gram_left.astype(jnp.bfloat16), gram_right.astype(jnp.bfloat16)])
        back = to_keepers(both)
        n_blocks = (s1 - s0) * n_dp
        left_terms.append(back[: b1 - b0])
        right_terms.append(back[n_blocks : n_blocks + b1 - b0])
        pieces.append(piece)
    piece = jnp.concatenate(pieces) if len(pieces) > 1 else pieces[0]
    half = jnp.einsum("cim,cmj->cij", piece, right_root, preferred_element_type=jnp.float32)
    half = half.astype(jnp.bfloat16)
    full_left = lax.all_gather(left_root, "group", axis=2, tiled=True)
    direction = jnp.einsum("cim,cmj->cij", full_left, half, preferred_element_type=jnp.float32)
    totals = lax.psum(
        jnp.concatenate([jnp.sum(direction * direction, axis=(1, 2)), dp_sums[:cap]]), "group"
    )
    direction_sq = totals[:cap]
    adam_owned = totals[cap:]
    ratio = jnp.sqrt(adam_owned / (direction_sq + EPS_GRAFT))
    scaled = (ratio[:, None, None] * direction).astype(jnp.bfloat16)
    scaled, norm_dp = lax.optimization_barrier((scaled, dp_sums[cap:]))
    block_step = to_keepers(scaled)[:count]
    norm_grad = lax.psum(norm_dp, "group").reshape(local_norm.shape)
    new_moment = jnp.concatenate(moments)
    left_term = jnp.concatenate(left_terms).astype(jnp.float32)
    right_term = jnp.concatenate(right_terms).astype(jnp.float32)
    new_left = 0.95 * left_stats + 0.05 * left_term
    new_right = 0.95 * right_stats + 0.05 * right_term
    new_norm_moment = 0.99 * norm_moment + 0.01 * norm_grad * norm_grad
    norm_step = norm_grad / (jnp.sqrt(new_norm_moment) + EPS_ADAM)
    return (block_step, new_moment, new_left, new_right, norm_step, new_norm_moment)


def solution(mesh):
    return jax.shard_map(
        on_device,
        mesh=mesh,
        in_specs=(
            P("group", None, "dp", None),
            P(None, "dp", "group"),
            P(None, "dp", "group"),
            P(None, "dp", "group"),
            P(None, "dp", "group"),
            P(None, "dp", "group"),
            P("dp", "group", None, None),
            P(),
        ),
        out_specs=(
            P(None, "dp", "group"),
            P(None, "dp", "group"),
            P(None, "dp", "group"),
            P(None, "dp", "group"),
            P(),
            P(),
        ),
        check_vma=False,
    )
```

profile of v0, /device:TPU:0, one launch (start us, length us, event | category | flops | bytes accessed | tf_op | source)
XLA Modules:
  0.0 602.5 jit_solution(5952788004856955438)
XLA Ops:
  7.2 11.1 %slice_bitcast_fusion.1 = f32[22,128,1024]{2,1,0:T(8,128)} fusion(f32[1,54,128,1024]{3,2,1,0:T(8,128)} %param.8), kind=kLoop, calls=%fused_computation.5 | loop fusion | bytes 23068672 | tf_op jit(solution)/shard_map/squeeze | solution.py:53
  18.3 13.7 %slice_bitcast_fusion = f32[32,128,1024]{2,1,0:T(8,128)} fusion(f32[1,54,128,1024]{3,2,1,0:T(8,128)} %param.8), kind=kLoop, calls=%fused_computation | loop fusion | bytes 33554432 | tf_op jit(solution)/shard_map/squeeze | solution.py:53
  37.8 7.0 %all-to-all-start = ((bf16[7,8,128,256]{3,2,0,1:T(8,128)(2,1)}), bf16[7,8,128,256]{3,2,0,1:T(8,128)(2,1)}, u32[]{:S(2)}, u32[]{:S(2)}) async-start(bf16[7,8,128,256]{3,2,0,1:T(8,128)(2,1)} %copy.26), calls=%async_computation.1 | async-start | bytes 7340032 | tf_op jit(solution)/shard_map/all_to_all | solution.py:45
  44.8 68.5 %reduce-scatter.5.cloned.1.call-done = f32[22,128,256]{2,1,0:T(8,128)} async-done(((f32[22,128,1024]{2,1,0:T(8,128)}), f32[22,128,256]{2,1,0:T(8,128)}) %reduce-scatter.5.cloned.1.call-update) | async-done | bytes 2883600 | tf_op jit(solution)/shard_map/reduce_scatter | solution.py:53
  113.3 6.9 %fusion.11 = (f32[22,128,256]{2,1,0:T(8,128)}, f32[22]{0:T(128)S(1)}, bf16[22,128,256]{2,1,0:T(8,128)(2,1)S(1)}) fusion(f32[22,128,256]{2,1,0:T(8,128)} %reduce-scatter.5.cloned.1.call-done, f32[54,128,256]{2,1,0:T(8,128)} %param.9), kind=kLoop, calls=%fused_computation.19 | loop fusion | flops 6488042 | bytes 10092632 | tf_op jit(solution)/shard_map/add | solution.py:59
  136.1 31.3 %all-to-all-done.4 = bf16[3,8,128,256]{3,2,0,1:T(8,128)(2,1)S(1)} async-done(((bf16[3,8,128,256]{3,2,0,1:T(8,128)(2,1)}), bf16[3,8,128,256]{3,2,0,1:T(8,128)(2,1)S(1)}, u32[]{:S(2)}, u32[]{:S(2)}) %all-to-all-start.4) | async-done | bytes 1572896 | tf_op jit(solution)/shard_map/all_to_all | solution.py:35
  173.4 68.7 %reduce-scatter.3.cloned.1.call-done = f32[32,128,256]{2,1,0:T(8,128)} async-done(((f32[32,128,1024]{2,1,0:T(8,128)}), f32[32,128,256]{2,1,0:T(8,128)}) %reduce-scatter.3.cloned.1.call-update) | async-done | bytes 4194320 | tf_op jit(solution)/shard_map/reduce_scatter | solution.py:53
  244.6 8.8 %all-to-all-done.1 = bf16[7,8,128,256]{3,2,0,1:T(8,128)(2,1)} async-done(((bf16[7,8,128,256]{3,2,0,1:T(8,128)(2,1)}), bf16[7,8,128,256]{3,2,0,1:T(8,128)(2,1)}, u32[]{:S(2)}, u32[]{:S(2)}) %all-to-all-start.1) | async-done | bytes 3670048 | tf_op jit(solution)/shard_map/all_to_all | solution.py:45
  253.5 51.8 %all_to_all.44 = bf16[4,8,128,256]{3,2,0,1:T(8,128)(2,1)S(1)} all-to-all(bf16[4,8,128,256]{3,2,0,1:T(8,128)(2,1)S(1)} %copy.30), channel_id=1, replica_groups=mesh['dp'=8,'group'=4] {'dp'}, dimensions={1} | all-to-all | bytes 4194304 | tf_op jit(solution)/shard_map/all_to_all | solution.py:35
  311.9 7.5 %fusion.4 = (f32[32,128,256]{2,1,0:T(8,128)}, f32[32]{0:T(128)S(1)}) fusion(f32[32,128,256]{2,1,0:T(8,128)} %reduce-scatter.3.cloned.1.call-done, f32[54,128,256]{2,1,0:T(8,128)} %param.9), kind=kLoop, calls=%fused_computation.13 | loop fusion | flops 8388576 | bytes 12583040 | tf_op jit(solution)/shard_map/add | solution.py:59
  324.0 5.3 convolution_convert_fusion.1
  333.5 5.7 all-to-all-start.7
  339.4 26.1 %all-gather.6.cloned.1.call-done = bf16[4,1024,1024]{2,1,0:T(8,128)(2,1)} async-done(((bf16[4,1024,256]{2,1,0:T(8,128)(2,1)}), bf16[4,1024,1024]{2,1,0:T(8,128)(2,1)}) %all-gather.6.cloned.1.call-update) | async-done | bytes 8388624 | tf_op jit(solution)/shard_map/all_gather | solution.py:75
  365.5 6.5 %fusion.14 = bf16[4,1024,256]{2,1,0:T(8,128)(2,1)S(1)} fusion(bf16[4,1024,1024]{2,1,0:T(8,128)(2,1)} %all-gather.6.cloned.1.call-done, s32[]{:T(128)S(6)} %select_n.4), kind=kOutput, calls=%fused_computation.23 | convolution fusion | flops 2148532224 | bytes 12582916 | tf_op jit(solution)/shard_map/cim,cjm->cij/dot_general | solution.py:79
  372.0 7.4 %convolution_convert_fusion = bf16[4,1024,256]{2,1,0:T(8,128)(2,1)S(1)} fusion(bf16[4,1024,1024]{2,1,0:T(8,128)(2,1)} %all-gather.6.cloned.1.call-done, bf16[4,1024,256]{2,1,0:T(8,128)(2,1)S(1)} %bitcast.42), kind=kOutput, calls=%fused_computation.24 | convolution fusion | flops 2148532224 | bytes 12582912 | tf_op jit(solution)/shard_map/cim,cij->cmj/dot_general | solution.py:80
  382.4 25.9 %all-to-all-done.7 = bf16[6,8,128,256]{3,2,0,1:T(8,128)(2,1)S(1)} async-done(((bf16[6,8,128,256]{3,2,0,1:T(8,128)(2,1)}), bf16[6,8,128,256]{3,2,0,1:T(8,128)(2,1)S(1)}, u32[]{:S(2)}, u32[]{:S(2)}) %all-to-all-start.7) | async-done | bytes 3145760 | tf_op jit(solution)/shard_map/all_to_all | solution.py:40
  417.5 46.0 %all-gather.4.cloned.1.call-done = bf16[7,1024,1024]{2,1,0:T(8,128)(2,1)} async-done(((bf16[7,1024,256]{2,1,0:T(8,128)(2,1)}), bf16[7,1024,1024]{2,1,0:T(8,128)(2,1)}) %all-gather.4.cloned.1.call-update) | async-done | bytes 14680080 | tf_op jit(solution)/shard_map/all_gather | solution.py:90
  463.6 17.7 %multiply_reduce_fusion = (f32[7]{0:T(128)S(1)}, f32[7,1024,256]{2,1,0:T(8,128)}) fusion(bf16[7,1024,1024]{2,1,0:T(8,128)(2,1)} %all-gather.4.cloned.1.call-done, bf16[7,1024,256]{2,1,0:T(8,128)(2,1)} %bitcast.48, bf16[3,1024,1024]{2,1,0:T(8,128)(2,1)} %all-gather.8.cloned.1.call-done, bf16[4,1024,1024]{2,1,0:T(8,128)(2,1)} %all-gather.6.cloned.1.call-done), kind=kOutput, calls=%fused_computation.7 | convolution fusion | flops 7529037824 | bytes 40370204 | tf_op jit(solution)/shard_map/cim,cmj->cij/dot_general | solution.py:91
  481.3 5.9 psum.14
  493.3 12.2 %all-to-all-done.6 = bf16[8,8,128,256]{3,2,0,1:T(8,128)(2,1)} async-done(((bf16[8,8,128,256]{3,2,0,1:T(8,128)(2,1)}), bf16[8,8,128,256]{3,2,0,1:T(8,128)(2,1)}, u32[]{:S(2)}, u32[]{:S(2)}) %all-to-all-start.6) | async-done | bytes 4194336 | tf_op jit(solution)/shard_map/all_to_all | solution.py:40
  510.1 6.8 %pad_maximum_fusion = f32[54,128,256]{2,1,0:T(8,128)} fusion(f32[22,128,256]{2,1,0:T(8,128)} %get-tuple-element.26, f32[32,128,256]{2,1,0:T(8,128)} %get-tuple-element.24), kind=kLoop, calls=%fused_computation.8 | loop fusion | flops 1769472 | bytes 14155776 | tf_op jit(solution)/shard_map/concatenate | solution.py:102
  517.3 10.9 %psum.15 = f32[2,2048]{1,0:T(2,128)S(1)} all-reduce(f32[2,2048]{1,0:T(2,128)S(1)} %reshape.78), channel_id=1, replica_groups=mesh['dp'=8,'group'=4] {'group'}, use_global_device_ids=true, to_apply=%region_7.8 | all-reduce | flops 4096 | bytes 32768 | tf_op jit(solution)/shard_map/psum | solution.py:101
  533.7 8.7 %multiply_add_fusion = (f32[54,128,256]{2,1,0:T(8,128)}, f32[54,128,256]{2,1,0:T(8,128)}) fusion(f32[54,128,256]{2,1,0:T(8,128)S(1)} %bitcast.44, bf16[22,128,256]{2,1,0:T(8,128)(2,1)S(1)} %get-tuple-element.30, bf16[32,128,256]{2,1,0:T(8,128)(2,1)S(1)} %bitcast.38, bf16[22,128,256]{2,1,0:T(8,128)(2,1)S(1)} %get-tuple-element.31, ...), kind=kLoop, calls=%fused_computation.9 | loop fusion | flops 17694720 | bytes 35389440 | tf_op jit(solution)/shard_map/add | solution.py:106
  542.5 48.8 %all-to-all-done.5 = bf16[7,8,128,256]{3,2,0,1:T(8,128)(2,1)} async-done(((bf16[7,8,128,256]{3,2,0,1:T(8,128)(2,1)}), bf16[7,8,128,256]{3,2,0,1:T(8,128)(2,1)}, u32[]{:S(2)}, u32[]{:S(2)}) %all-to-all-start.5) | async-done | bytes 3670048 | tf_op jit(solution)/shard_map/all_to_all | solution.py:40
  (78 shorter events, 79.0 us)
Async XLA Ops:
  7.2 106.2 %reduce-scatter.5.cloned.1.call-start = ((), (), s32[]{:S(2)}) async-start(), calls=%async_computation.12 | async-start | bytes 14417920 | tf_op jit(solution)/shard_map/reduce_scatter | solution.py:53
  18.3 223.8 %reduce-scatter.3.cloned.1.call-start = ((), (), s32[]{:S(2)}) async-start(), calls=%async_computation.10 | async-start | bytes 20971520 | tf_op jit(solution)/shard_map/reduce_scatter | solution.py:53
  32.0 2.8 copy-start.2
  37.8 88.8 %all-to-all-start = ((bf16[7,8,128,256]{3,2,0,1:T(8,128)(2,1)}), bf16[7,8,128,256]{3,2,0,1:T(8,128)(2,1)}, u32[]{:S(2)}, u32[]{:S(2)}) async-start(bf16[7,8,128,256]{3,2,0,1:T(8,128)(2,1)} %copy.26), calls=%async_computation.1 | async-start | bytes 7340032 | tf_op jit(solution)/shard_map/all_to_all | solution.py:45
  126.7 40.8 %all-to-all-start.4 = ((bf16[3,8,128,256]{3,2,0,1:T(8,128)(2,1)}), bf16[3,8,128,256]{3,2,0,1:T(8,128)(2,1)S(1)}, u32[]{:S(2)}, u32[]{:S(2)}) async-start(bf16[3,8,128,256]{3,2,0,1:T(8,128)(2,1)} %copy.32), calls=%async_computation.6 | async-start | bytes 3145728 | tf_op jit(solution)/shard_map/all_to_all | solution.py:35
  167.5 85.9 %all-to-all-start.1 = ((bf16[7,8,128,256]{3,2,0,1:T(8,128)(2,1)}), bf16[7,8,128,256]{3,2,0,1:T(8,128)(2,1)}, u32[]{:S(2)}, u32[]{:S(2)}) async-start(bf16[7,8,128,256]{3,2,0,1:T(8,128)(2,1)} %copy.27), calls=%async_computation.2 | async-start | bytes 7340032 | tf_op jit(solution)/shard_map/all_to_all | solution.py:45
  172.0 152.0 %all-gather.8.cloned.1.call-start = ((), (), s32[]{:S(2)}) async-start(), calls=%async_computation.14 | async-start | bytes 7864320 | tf_op jit(solution)/shard_map/all_gather | solution.py:75
  173.3 192.2 %all-gather.6.cloned.1.call-start = ((), (), s32[]{:S(2)}) async-start(), calls=%async_computation.13 | async-start | bytes 10485760 | tf_op jit(solution)/shard_map/all_gather | solution.py:75
  306.8 156.8 %all-gather.4.cloned.1.call-start = ((), (), s32[]{:S(2)}) async-start(), calls=%async_computation.11 | async-start | bytes 18350080 | tf_op jit(solution)/shard_map/all_gather | solution.py:90
  311.1 0.7 copy-start.4
  311.9 12.1 %copy-start.1 = (bf16[3,8,128,256]{3,2,1,0:T(8,128)(2,1)S(1)}, bf16[3,8,128,256]{3,2,1,0:T(8,128)(2,1)}, u32[]{:S(2)}) copy-start(bf16[3,8,128,256]{3,2,1,0:T(8,128)(2,1)} %copy.33) | copy-start | bytes 4718596
  320.4 13.1 %all-to-all-start.2 = ((f32[8,1,4103]{2,1,0:T(1,128)}), f32[8,1,4103]{2,1,0:T(1,128)S(1)}, u32[]{:S(2)}, u32[]{:S(2)}) async-start(f32[8,1,4103]{2,1,0:T(1,128)} %all_to_all.29), calls=%async_computation.4 | async-start | bytes 270336 | tf_op jit(solution)/shard_map/all_to_all | solution.py:69
  324.0 5.4 copy-start.6
  333.5 74.8 %all-to-all-start.7 = ((bf16[6,8,128,256]{3,2,0,1:T(8,128)(2,1)}), bf16[6,8,128,256]{3,2,0,1:T(8,128)(2,1)S(1)}, u32[]{:S(2)}, u32[]{:S(2)}) async-start(bf16[6,8,128,256]{3,2,0,1:T(8,128)(2,1)} %copy.41), calls=%async_computation.9 | async-start | bytes 6291456 | tf_op jit(solution)/shard_map/all_to_all | solution.py:40
  339.3 78.1 %copy-start.3 = (f32[4103]{0:T(1024)}, f32[4103]{0:T(1024)S(1)}, u32[]{:S(2)}) copy-start(f32[4103]{0:T(1024)S(1)} %reduce_sum.38) | copy-start | bytes 49240
  365.5 6.5 %copy-start = (bf16[4,8,128,256]{3,2,1,0:T(8,128)(2,1)S(1)}, bf16[4,8,128,256]{3,2,1,0:T(8,128)(2,1)}, u32[]{:S(2)}) copy-start(bf16[4,8,128,256]{3,2,1,0:T(8,128)(2,1)} %copy.31) | copy-start | bytes 6291460
  408.3 97.2 %all-to-all-start.6 = ((bf16[8,8,128,256]{3,2,0,1:T(8,128)(2,1)}), bf16[8,8,128,256]{3,2,0,1:T(8,128)(2,1)}, u32[]{:S(2)}, u32[]{:S(2)}) async-start(bf16[8,8,128,256]{3,2,0,1:T(8,128)(2,1)} %copy.38), calls=%async_computation.8 | async-start | bytes 8388608 | tf_op jit(solution)/shard_map/all_to_all | solution.py:40
  463.5 17.7 %slice-start.2 = ((f32[4103]{0:T(1024)}), f32[7]{0:T(128)S(1)}, s32[]{:S(2)}) async-start(f32[4103]{0:T(1024)} %copy-done.3), calls=%async_computation.17 | async-start | bytes 1024 | tf_op jit(solution)/shard_map/slice | solution.py:93
  505.6 85.7 %all-to-all-start.5 = ((bf16[7,8,128,256]{3,2,0,1:T(8,128)(2,1)}), bf16[7,8,128,256]{3,2,0,1:T(8,128)(2,1)}, u32[]{:S(2)}, u32[]{:S(2)}) async-start(bf16[7,8,128,256]{3,2,0,1:T(8,128)(2,1)} %copy.35), calls=%async_computation.7 | async-start | bytes 7340032 | tf_op jit(solution)/shard_map/all_to_all | solution.py:40
  517.1 11.1 %copy-start.5 = (f32[2,2048]{1,0:T(2,128)S(1)}, f32[2,2048]{1,0:T(2,128)}, u32[]{:S(2)}) copy-start(f32[2,2048]{1,0:T(2,128)} %param.15) | copy-start | bytes 49156
  528.9 3.5 slice-start
  531.8 2.0 slice-start.1
Sparse Core Ops, SparseCore 0:
  18.4 94.8 reduce-scatter.4
  115.9 126.1 reduce-scatter.2
  244.3 47.2 all-gather.7
  306.9 58.5 all-gather.5
  367.5 95.9 all-gather.3
where the time goes:
time: 604 us; the launch traced here: 602 us
  waiting for transfers between devices  342 us (57%)
  blocking collectives  68.6 us (11%)
  local copies, waits for them, and re-layouts  67.7 us (11%)
  matrix products  38.8 us (6%)
  other arithmetic  37.8 us (6%)
  starting transfers between devices  33.9 us (6%)
  between operations  14 us (2%)
    reduce_scatter x2, waiting for transfers between devices, on_device(): lax.psum_scatter(partials[0, b0:b1], 'group', scatter_dimension=2, tiled=...  137 us
    all_to_all x3, waiting for transfers between devices, to_keepers(): lax.all_to_all(owned.reshape(n_slots, n_dp, rows, quarter), 'dp', 1, 1, t...  86.9 us
    all_to_all x1, blocking collectives, to_owners(): lax.all_to_all(padded.reshape(n_slots, n_dp, rows, quarter), 'dp', 1, 1,...  51.8 us
    all_gather x1, waiting for transfers between devices, on_device(): full_left = lax.all_gather(left_root, 'group', axis=2, tiled=True)  46 us
    all_to_all x1, waiting for transfers between devices, to_owners(): lax.all_to_all(padded.reshape(n_slots, n_dp, rows, quarter), 'dp', 1, 1,...  31.3 us
    all_gather x2, waiting for transfers between devices, on_device(): piece = lax.all_gather(mine, 'group', axis=2, tiled=True)  26.2 us
    squeeze x2, local copies, waits for them, and re-layouts, on_device(): partials[0, b0:b1]  24.7 us
    dot_general x1, matrix products, on_device(): jnp.einsum('cim,cmj->cij', full_left, half, preferred_element_type=jnp.fl...  17.7 us
  transfers between devices with their start and end apart: 12, of which 10 were waited for; matrix products, arithmetic and copies ran while one was open for 20% of the time, Pallas kernels for 0%

commit v1 on v0

--- a/solution.py
+++ b/solution.py
@@ -5,6 +5,28 @@
 
 EPS_ADAM = 1e-08
 EPS_GRAFT = 1e-06
+
+
+def laid_out(pieces, dim):
+    shape = list(pieces.shape[1:])
+    shape[dim] *= pieces.shape[0]
+    return jnp.moveaxis(pieces, 0, dim).reshape(shape)
+
+
+def collect(shard, axis, dim):
+    length = lax.axis_size(axis)
+    pairs = [(i, (i + 1) % length) for i in range(length)]
+    back = [(b, a) for a, b in pairs]
+    lower, upper = ([], [])
+    for turn in range(length - 1):
+        if turn % 2 == 0:
+            lower.append(lax.ppermute(lower[-1] if lower else shard, axis, pairs))
+        else:
+            upper.append(lax.ppermute(upper[-1] if upper else shard, axis, back))
+    blocks = jnp.stack([*lower[::-1], shard, *upper])
+    shift = lax.axis_index(axis) - len(lower)
+    blocks = blocks[(jnp.arange(length) - shift) % length]
+    return laid_out(blocks, dim)
 
 
 def on_device(
@@ -72,7 +94,7 @@
     for (s0, s1), grad_low in zip(bounds, grads):
         b0, b1 = (s0 * n_dp, min(s1 * n_dp, count))
         mine = to_owners(grad_low, s1 - s0)
-        piece = lax.all_gather(mine, "group", axis=2, tiled=True)
+        piece = collect(mine, "group", 2)
         if s0 == 0:
             dp_sums, piece = lax.optimization_barrier((dp_sums, piece))
         own_rows = lax.dynamic_slice_in_dim(piece, lower, quarter, 1)

time: 604 us -> 730 us (1.21)
  waiting for transfers between devices: 342 us -> 421 us
  local copies, waits for them, and re-layouts: 67.7 us -> 99.7 us
  other arithmetic: 37.8 us -> 55.7 us
  blocking collectives: 68.6 us -> 59.5 us
    ppermute x0 -> x6, waiting for transfers between devices: none -> 131 us  [the longest x4 117 us: collect(): lower.append(lax.ppermute(lower[-1] if lower else shard, axis, pairs))]
    all_to_all x2, waiting for transfers between devices: 13.8 us -> 141 us  [roots_to_owners(): lax.all_to_all(padded.reshape(cap, n_dp, rows, quarter), 'dp', 1, 1, tile...]
    reduce_scatter x2, waiting for transfers between devices: 137 us -> 42.4 us  [on_device(): lax.psum_scatter(partials[0, b0:b1], 'group', scatter_dimension=2, tiled=...]
    all_gather x1, waiting for transfers between devices: 46 us -> 0.01 us  [on_device(): full_left = lax.all_gather(left_root, 'group', axis=2, tiled=True)]
    all_to_all x1, waiting for transfers between devices: 31.3 us -> 0.01 us  [to_owners(): lax.all_to_all(padded.reshape(n_slots, n_dp, rows, quarter), 'dp', 1, 1,...]
    all_gather x2 -> x0, waiting for transfers between devices: 26.2 us -> none  [on_device(): piece = lax.all_gather(mine, 'group', axis=2, tiled=True)]
    gather x0 -> x4, local copies, waits for them, and re-layouts: none -> 20.1 us  [collect(): blocks = blocks[(jnp.arange(length) - shift) % length]]
    all_to_all x3, waiting for transfers between devices: 86.9 us -> 106 us  [to_keepers(): lax.all_to_all(owned.reshape(n_slots, n_dp, rows, quarter), 'dp', 1, 1, t...]
  transfers between devices with their start and end apart: 12 -> 16, of which waited for: 10 -> 12; matrix products, arithmetic and copies ran while one was open for 20% -> 23% of each run, Pallas kernels for 0% -> 0%
where the time goes in v1:
time: 730 us; the launch traced here: 728 us
  waiting for transfers between devices  421 us (58%)
  local copies, waits for them, and re-layouts  99.7 us (14%)
  blocking collectives  59.5 us (8%)
  other arithmetic  55.7 us (8%)
  matrix products  40.1 us (5%)
  starting transfers between devices  38.3 us (5%)
  between operations  14 us (2%)
    all_to_all x2, waiting for transfers between devices, roots_to_owners(): lax.all_to_all(padded.reshape(cap, n_dp, rows, quarter), 'dp', 1, 1, tile...  141 us
    ppermute x4, waiting for transfers between devices, collect(): lower.append(lax.ppermute(lower[-1] if lower else shard, axis, pairs))  117 us
    all_to_all x3, waiting for transfers between devices, to_keepers(): lax.all_to_all(owned.reshape(n_slots, n_dp, rows, quarter), 'dp', 1, 1, t...  106 us
    reduce_scatter x2, waiting for transfers between devices, on_device(): lax.psum_scatter(partials[0, b0:b1], 'group', scatter_dimension=2, tiled=...  42.4 us
    all_to_all x1, blocking collectives, to_owners(): lax.all_to_all(padded.reshape(n_slots, n_dp, rows, quarter), 'dp', 1, 1,...  42.3 us
    squeeze x2, local copies, waits for them, and re-layouts, on_device(): partials[0, b0:b1]  24.5 us
    gather x4, local copies, waits for them, and re-layouts, collect(): blocks = blocks[(jnp.arange(length) - shift) % length]  20.1 us
    dot_general x1, matrix products, on_device(): jnp.einsum('cim,cmj->cij', full_left, half, preferred_element_type=jnp.fl...  17.7 us
  transfers between devices with their start and end apart: 16, of which 12 were waited for; matrix products, arithmetic and copies ran while one was open for 23% of the time, Pallas kernels for 0%

profile of v1, /device:TPU:0, one launch (start us, length us, event | category | flops | bytes accessed | tf_op | source)
XLA Modules:
  0.0 728.3 jit_solution(16271781148391546883)
XLA Ops:
  7.2 11.8 %slice_bitcast_fusion = f32[32,128,1024]{2,1,0:T(8,128)} fusion(f32[1,54,128,1024]{3,2,1,0:T(8,128)} %param.8), kind=kLoop, calls=%fused_computation.3 | loop fusion | bytes 33554432 | tf_op jit(solution)/shard_map/squeeze | solution.py:75
  19.1 12.7 %slice_bitcast_fusion.1 = f32[22,128,1024]{2,1,0:T(8,128)} fusion(f32[1,54,128,1024]{3,2,1,0:T(8,128)} %param.8), kind=kLoop, calls=%fused_computation.8 | loop fusion | bytes 23068672 | tf_op jit(solution)/shard_map/squeeze | solution.py:75
  37.6 7.5 %all-to-all-start = ((bf16[7,8,128,256]{3,2,0,1:T(8,128)(2,1)}), bf16[7,8,128,256]{3,2,0,1:T(8,128)(2,1)}, u32[]{:S(2)}, u32[]{:S(2)}) async-start(bf16[7,8,128,256]{3,2,0,1:T(8,128)(2,1)} %copy.32), calls=%async_computation.1 | async-start | bytes 7340032 | tf_op jit(solution)/shard_map/all_to_all | solution.py:67
  47.8 79.1 %all-to-all-done = bf16[7,8,128,256]{3,2,0,1:T(8,128)(2,1)} async-done(((bf16[7,8,128,256]{3,2,0,1:T(8,128)(2,1)}), bf16[7,8,128,256]{3,2,0,1:T(8,128)(2,1)}, u32[]{:S(2)}, u32[]{:S(2)}) %all-to-all-start) | async-done | bytes 3670048 | tf_op jit(solution)/shard_map/all_to_all | solution.py:67
  131.5 16.6 %reduce-scatter.3.cloned.1.call-done = f32[32,128,256]{2,1,0:T(8,128)} async-done(((f32[32,128,1024]{2,1,0:T(8,128)}), f32[32,128,256]{2,1,0:T(8,128)}) %reduce-scatter.3.cloned.1.call-update) | async-done | bytes 4194320 | tf_op jit(solution)/shard_map/reduce_scatter | solution.py:75
  150.5 62.3 %all-to-all-done.1 = bf16[7,8,128,256]{3,2,0,1:T(8,128)(2,1)} async-done(((bf16[7,8,128,256]{3,2,0,1:T(8,128)(2,1)}), bf16[7,8,128,256]{3,2,0,1:T(8,128)(2,1)}, u32[]{:S(2)}, u32[]{:S(2)}) %all-to-all-start.1) | async-done | bytes 3670048 | tf_op jit(solution)/shard_map/all_to_all | solution.py:67
  217.2 25.8 %reduce-scatter.5.cloned.1.call-done = f32[22,128,256]{2,1,0:T(8,128)} async-done(((f32[22,128,1024]{2,1,0:T(8,128)}), f32[22,128,256]{2,1,0:T(8,128)}) %reduce-scatter.5.cloned.1.call-update) | async-done | bytes 2883600 | tf_op jit(solution)/shard_map/reduce_scatter | solution.py:75
  243.0 6.8 fusion.11
  250.1 42.3 %all_to_all.44 = bf16[3,8,128,256]{3,2,0,1:T(8,128)(2,1)S(1)} all-to-all(bf16[3,8,128,256]{3,2,0,1:T(8,128)(2,1)S(1)} %copy.40), channel_id=1, replica_groups=mesh['dp'=8,'group'=4] {'dp'}, dimensions={1} | all-to-all | bytes 3145728 | tf_op jit(solution)/shard_map/all_to_all | solution.py:57
  300.6 61.8 %collective-permute-done.3 = bf16[3,1024,256]{2,1,0:T(8,128)(2,1)} collective-permute-done((bf16[3,1024,256]{2,1,0:T(8,128)(2,1)}, bf16[3,1024,256]{2,1,0:T(8,128)(2,1)}, u32[]{:S(2)}, u32[]{:S(2)}) %collective-permute-start.3) | collective-permute-done | bytes 1572896 | tf_op jit(solution)/shard_map/ppermute | solution.py:23
  368.2 19.1 %collective-permute-done.4 = bf16[3,1024,256]{2,1,0:T(8,128)(2,1)} collective-permute-done((bf16[3,1024,256]{2,1,0:T(8,128)(2,1)}, bf16[3,1024,256]{2,1,0:T(8,128)(2,1)}, u32[]{:S(2)}, u32[]{:S(2)}) %collective-permute-start.4) | collective-permute-done | bytes 1572896 | tf_op jit(solution)/shard_map/ppermute | solution.py:23
  387.3 6.5 pad_maximum_fusion.2
  426.6 22.0 %collective-permute-done = bf16[4,1024,256]{2,1,0:T(8,128)(2,1)} collective-permute-done((bf16[4,1024,256]{2,1,0:T(8,128)(2,1)}, bf16[4,1024,256]{2,1,0:T(8,128)(2,1)}, u32[]{:S(2)}, u32[]{:S(2)}) %collective-permute-start) | collective-permute-done | bytes 2097184 | tf_op jit(solution)/shard_map/ppermute | solution.py:23
  461.2 8.5 %collective-permute-done.2 = bf16[4,1024,256]{2,1,0:T(8,128)(2,1)} collective-permute-done((bf16[4,1024,256]{2,1,0:T(8,128)(2,1)}, bf16[4,1024,256]{2,1,0:T(8,128)(2,1)}, u32[]{:S(2)}, u32[]{:S(2)}) %collective-permute-start.2) | collective-permute-done | bytes 2097184 | tf_op jit(solution)/shard_map/ppermute | solution.py:25
  469.7 14.1 %collective-permute-done.1 = bf16[4,1024,256]{2,1,0:T(8,128)(2,1)} collective-permute-done((bf16[4,1024,256]{2,1,0:T(8,128)(2,1)}, bf16[4,1024,256]{2,1,0:T(8,128)(2,1)}, u32[]{:S(2)}, u32[]{:S(2)}) %collective-permute-start.1) | collective-permute-done | bytes 2097184 | tf_op jit(solution)/shard_map/ppermute | solution.py:23
  501.9 7.5 %maximum_bitcast_fusion = bf16[4,4,128,8,256]{4,3,2,1,0:T(8,128)(2,1)} fusion(bf16[4,4,512,256]{3,2,1,0:T(8,128)(2,1)} %gather_fusion.2, bf16[4,4,512,256]{3,2,1,0:T(8,128)(2,1)} %gather_fusion.1), kind=kLoop, calls=%fused_computation.10 | loop fusion | flops 16777216 | bytes 16777216
  509.4 7.8 %copy.58 = bf16[4,4,128,8,256]{4,3,0,2,1:T(8,128)(2,1)} copy(bf16[4,4,128,8,256]{4,3,2,1,0:T(8,128)(2,1)} %maximum_bitcast_fusion) | data formatting | bytes 16777216 | tf_op jit(solution)/shard_map/reshape | solution.py:13
  517.2 6.5 fusion.14
  543.9 17.7 %multiply_reduce_fusion = (f32[7]{0:T(128)S(1)}, f32[7,1024,256]{2,1,0:T(8,128)}) fusion(bf16[7,1024,1024]{2,1,0:T(8,128)(2,1)} %all-gather.2.cloned.1.call-done, bf16[7,1024,256]{2,1,0:T(8,128)(2,1)} %bitcast.68, bf16[3,1024,1024]{2,1,0:T(8,128)(2,1)} %bitcast.66, bf16[4,1024,1024]{2,1,0:T(8,128)(2,1)} %bitcast.60), kind=kOutput, calls=%fused_computation.12 | convolution fusion | flops 7529037824 | bytes 40370204 | tf_op jit(solution)/shard_map/cim,cmj->cij/dot_general | solution.py:113
  574.1 57.1 %all-to-all-done.6 = bf16[8,8,128,256]{3,2,0,1:T(8,128)(2,1)} async-done(((bf16[8,8,128,256]{3,2,0,1:T(8,128)(2,1)}), bf16[8,8,128,256]{3,2,0,1:T(8,128)(2,1)}, u32[]{:S(2)}, u32[]{:S(2)}) %all-to-all-start.6) | async-done | bytes 4194336 | tf_op jit(solution)/shard_map/all_to_all | solution.py:62
  635.7 6.8 pad_maximum_fusion.1
  647.8 8.8 %multiply_add_fusion = (f32[54,128,256]{2,1,0:T(8,128)}, f32[54,128,256]{2,1,0:T(8,128)}) fusion(f32[54,128,256]{2,1,0:T(8,128)S(1)} %bitcast.63, bf16[22,128,256]{2,1,0:T(8,128)(2,1)S(1)} %get-tuple-element.32, bf16[32,128,256]{2,1,0:T(8,128)(2,1)S(1)} %bitcast.57, bf16[22,128,256]{2,1,0:T(8,128)(2,1)S(1)} %get-tuple-element.33, ...), kind=kLoop, calls=%fused_computation.14 | loop fusion | flops 17694720 | bytes 35389440 | tf_op jit(solution)/shard_map/add | solution.py:128
  656.6 10.9 %psum.15 = f32[2,2048]{1,0:T(2,128)S(1)} all-reduce(f32[2,2048]{1,0:T(2,128)S(1)} %reshape.135), channel_id=1, replica_groups=mesh['dp'=8,'group'=4] {'group'}, use_global_device_ids=true, to_apply=%region_7.8 | all-reduce | flops 4096 | bytes 32768 | tf_op jit(solution)/shard_map/psum | solution.py:123
  668.2 48.9 %all-to-all-done.5 = bf16[7,8,128,256]{3,2,0,1:T(8,128)(2,1)} async-done(((bf16[7,8,128,256]{3,2,0,1:T(8,128)(2,1)}), bf16[7,8,128,256]{3,2,0,1:T(8,128)(2,1)}, u32[]{:S(2)}, u32[]{:S(2)}) %all-to-all-start.5) | async-done | bytes 3670048 | tf_op jit(solution)/shard_map/all_to_all | solution.py:62
  (99 shorter events, 145.5 us)
Async XLA Ops:
  7.2 140.9 %reduce-scatter.3.cloned.1.call-start = ((), (), s32[]{:S(2)}) async-start(), calls=%async_computation.10 | async-start | bytes 20971520 | tf_op jit(solution)/shard_map/reduce_scatter | solution.py:75
  19.0 224.0 %reduce-scatter.5.cloned.1.call-start = ((), (), s32[]{:S(2)}) async-start(), calls=%async_computation.12 | async-start | bytes 14417920 | tf_op jit(solution)/shard_map/reduce_scatter | solution.py:75
  37.6 7.5 %copy-start.4 = (bf16[54,128,256]{2,1,0:T(8,128)(2,1)S(1)}, bf16[54,128,256]{2,1,0:T(8,128)(2,1)}, u32[]{:S(2)}) copy-start(bf16[54,128,256]{2,1,0:T(8,128)(2,1)} %param.13) | copy-start | bytes 10616836
  37.6 89.3 %all-to-all-start = ((bf16[7,8,128,256]{3,2,0,1:T(8,128)(2,1)}), bf16[7,8,128,256]{3,2,0,1:T(8,128)(2,1)}, u32[]{:S(2)}, u32[]{:S(2)}) async-start(bf16[7,8,128,256]{3,2,0,1:T(8,128)(2,1)} %copy.32), calls=%async_computation.1 | async-start | bytes 7340032 | tf_op jit(solution)/shard_map/all_to_all | solution.py:67
  126.9 85.9 %all-to-all-start.1 = ((bf16[7,8,128,256]{3,2,0,1:T(8,128)(2,1)}), bf16[7,8,128,256]{3,2,0,1:T(8,128)(2,1)}, u32[]{:S(2)}, u32[]{:S(2)}) async-start(bf16[7,8,128,256]{3,2,0,1:T(8,128)(2,1)} %copy.33), calls=%async_computation.2 | async-start | bytes 7340032 | tf_op jit(solution)/shard_map/all_to_all | solution.py:67
  131.4 412.5 %all-gather.2.cloned.1.call-start = ((), (), s32[]{:S(2)}) async-start(), calls=%async_computation.11 | async-start | bytes 18350080 | tf_op jit(solution)/shard_map/all_gather | solution.py:112
  293.7 68.7 %collective-permute-start.3 = (bf16[3,1024,256]{2,1,0:T(8,128)(2,1)}, bf16[3,1024,256]{2,1,0:T(8,128)(2,1)}, u32[]{:S(2)}, u32[]{:S(2)}) collective-permute-start(bf16[3,1024,256]{2,1,0:T(8,128)(2,1)} %bitcast.15), channel_id=1, source_target_pairs={{0,1},{1,2},{2,3},{3,0},{4,5},{5,6},{6,7},{7,4},{8,9},{9,10},{10,1... | collective-permute-start | bytes 4718600 | tf_op jit(solution)/shard_map/ppermute | solution.py:23
  293.7 68.7 %copy-start.7 = (f32[1,1,2,2048]{3,2,1,0:T(2,128)S(1)}, f32[1,1,2,2048]{3,2,1,0:T(2,128)}, u32[]{:S(2)}) copy-start(f32[1,1,2,2048]{3,2,1,0:T(2,128)} %param.14) | copy-start | bytes 49156
  295.1 116.4 %all-to-all-start.3 = ((bf16[4,8,128,256]{3,2,0,1:T(8,128)(2,1)}), bf16[4,8,128,256]{3,2,0,1:T(8,128)(2,1)S(1)}, u32[]{:S(2)}, u32[]{:S(2)}) async-start(bf16[4,8,128,256]{3,2,0,1:T(8,128)(2,1)} %copy.36), calls=%async_computation.5 | async-start | bytes 4194304 | tf_op jit(solution)/shard_map/all_to_all | solution.py:57
  298.7 69.5 %collective-permute-start.5 = (bf16[3,1024,256]{2,1,0:T(8,128)(2,1)}, bf16[3,1024,256]{2,1,0:T(8,128)(2,1)}, u32[]{:S(2)}, u32[]{:S(2)}) collective-permute-start(bf16[3,1024,256]{2,1,0:T(8,128)(2,1)} %bitcast.15), channel_id=1, source_target_pairs={{1,0},{2,1},{3,2},{0,3},{5,4},{6,5},{7,6},{4,7},{9,8},{10,9},{11,1... | collective-permute-start | bytes 4718600 | tf_op jit(solution)/shard_map/ppermute | solution.py:25
  362.4 24.9 %collective-permute-start.4 = (bf16[3,1024,256]{2,1,0:T(8,128)(2,1)}, bf16[3,1024,256]{2,1,0:T(8,128)(2,1)}, u32[]{:S(2)}, u32[]{:S(2)}) collective-permute-start(bf16[3,1024,256]{2,1,0:T(8,128)(2,1)} %collective-permute-done.3), channel_id=1, source_target_pairs={{0,1},{1,2},{2,3},{3,0},{4,5},{5,6},{6,7},{7,4},{8,9},{9,10},{10,1... | collective-permute-start | bytes 4718600 | tf_op jit(solution)/shard_map/ppermute | solution.py:23
  413.1 35.5 %collective-permute-start = (bf16[4,1024,256]{2,1,0:T(8,128)(2,1)}, bf16[4,1024,256]{2,1,0:T(8,128)(2,1)}, u32[]{:S(2)}, u32[]{:S(2)}) collective-permute-start(bf16[4,1024,256]{2,1,0:T(8,128)(2,1)} %bitcast.7), channel_id=1, source_target_pairs={{0,1},{1,2},{2,3},{3,0},{4,5},{5,6},{6,7},{7,4},{8,9},{9,10},{10,1... | collective-permute-start | bytes 6291464 | tf_op jit(solution)/shard_map/ppermute | solution.py:23
  421.0 34.9 %all-to-all-start.2 = ((f32[8,1,4103]{2,1,0:T(1,128)}), f32[8,1,4103]{2,1,0:T(1,128)S(1)}, u32[]{:S(2)}, u32[]{:S(2)}) async-start(f32[8,1,4103]{2,1,0:T(1,128)} %all_to_all.29), calls=%async_computation.4 | async-start | bytes 270336 | tf_op jit(solution)/shard_map/all_to_all | solution.py:91
  426.6 27.1 %copy-start.5 = (bf16[3,1024,256]{2,1,0:T(8,128)(2,1)S(1)}, bf16[3,1024,256]{2,1,0:T(8,128)(2,1)}, u32[]{:S(2)}) copy-start(bf16[3,1024,256]{2,1,0:T(8,128)(2,1)} %convolution_convert_fusion.1) | copy-start | bytes 4718596
  426.6 43.1 %collective-permute-start.2 = (bf16[4,1024,256]{2,1,0:T(8,128)(2,1)}, bf16[4,1024,256]{2,1,0:T(8,128)(2,1)}, u32[]{:S(2)}, u32[]{:S(2)}) collective-permute-start(bf16[4,1024,256]{2,1,0:T(8,128)(2,1)} %bitcast.7), channel_id=1, source_target_pairs={{1,0},{2,1},{3,2},{0,3},{5,4},{6,5},{7,6},{4,7},{9,8},{10,9},{11,1... | collective-permute-start | bytes 6291464 | tf_op jit(solution)/shard_map/ppermute | solution.py:25
  448.6 35.2 %collective-permute-start.1 = (bf16[4,1024,256]{2,1,0:T(8,128)(2,1)}, bf16[4,1024,256]{2,1,0:T(8,128)(2,1)}, u32[]{:S(2)}, u32[]{:S(2)}) collective-permute-start(bf16[4,1024,256]{2,1,0:T(8,128)(2,1)} %collective-permute-done), channel_id=1, source_target_pairs={{0,1},{1,2},{2,3},{3,0},{4,5},{5,6},{6,7},{7,4},{8,9},{9,10},{10,1... | collective-permute-start | bytes 6291464 | tf_op jit(solution)/shard_map/ppermute | solution.py:23
  456.0 78.1 %all-to-all-start.7 = ((bf16[6,8,128,256]{3,2,0,1:T(8,128)(2,1)}), bf16[6,8,128,256]{3,2,0,1:T(8,128)(2,1)S(1)}, u32[]{:S(2)}, u32[]{:S(2)}) async-start(bf16[6,8,128,256]{3,2,0,1:T(8,128)(2,1)} %copy.51), calls=%async_computation.9 | async-start | bytes 6291456 | tf_op jit(solution)/shard_map/all_to_all | solution.py:62
  461.2 82.7 %copy-start.6 = (f32[4103]{0:T(1024)}, f32[4103]{0:T(1024)S(1)}, u32[]{:S(2)}) copy-start(f32[4103]{0:T(1024)S(1)} %reduce_sum.38) | copy-start | bytes 49240
  517.2 6.5 copy-start.1
  534.1 97.2 %all-to-all-start.6 = ((bf16[8,8,128,256]{3,2,0,1:T(8,128)(2,1)}), bf16[8,8,128,256]{3,2,0,1:T(8,128)(2,1)}, u32[]{:S(2)}, u32[]{:S(2)}) async-start(bf16[8,8,128,256]{3,2,0,1:T(8,128)(2,1)} %copy.48), calls=%async_computation.8 | async-start | bytes 8388608 | tf_op jit(solution)/shard_map/all_to_all | solution.py:62
  543.9 17.7 %slice-start.2 = ((f32[4103]{0:T(1024)}), f32[7]{0:T(128)S(1)}, s32[]{:S(2)}) async-start(f32[4103]{0:T(1024)} %copy-done.6), calls=%async_computation.15 | async-start | bytes 1024 | tf_op jit(solution)/shard_map/slice | solution.py:115
  631.2 85.9 %all-to-all-start.5 = ((bf16[7,8,128,256]{3,2,0,1:T(8,128)(2,1)}), bf16[7,8,128,256]{3,2,0,1:T(8,128)(2,1)}, u32[]{:S(2)}, u32[]{:S(2)}) async-start(bf16[7,8,128,256]{3,2,0,1:T(8,128)(2,1)} %copy.45), calls=%async_computation.7 | async-start | bytes 7340032 | tf_op jit(solution)/shard_map/all_to_all | solution.py:62
  643.0 3.5 slice-start
  647.8 19.7 %copy-start.8 = (f32[2,2048]{1,0:T(2,128)S(1)}, f32[2,2048]{1,0:T(2,128)}, u32[]{:S(2)}) copy-start(f32[2,2048]{1,0:T(2,128)} %param.15) | copy-start | bytes 49156
  (4 other events, 10.4 us)
Sparse Core Ops, SparseCore 0:
  19.1 128.8 reduce-scatter.2
  150.8 92.1 reduce-scatter.4
  244.6 131.7 all-gather.1
